TPU v7x, 128 devices: a whole 4x4x4 slice. The times are simulated.
128 devices in a mesh: req: 32 (over x, z, core), tp: 4 (over y).
Axes of the slice: x: 4, y: 4, z: 4, core: 2. Of those that a mesh axis runs over, the one named last changes fastest.
Arguments:
- hidden: bfloat16 [8192, 2048], P('req', 'tp'), may hold values from -45 to 45
- routes: int32 [8192, 2], P('req'), may hold values from 0 to 7, all different within a row; in each aligned block of 256 rows (0 to 255, 256 to 511, ...) at most 128 rows name the same one
- route_weights: float32 [8192, 2], P('req'), may hold values from 0.2 to 1
- pre_gain: float32 [2048], replicated, may hold values from 0.1 to 1.9
- out_gain: float32 [2048], P('tp'), may hold values from 0.1 to 1.9
- gate_weight: bfloat16 [32, 2048, 5632], P('req', None, 'tp'), as said below
- up_weight: bfloat16 [32, 2048, 5632], P('req', None, 'tp'), as said below
- down_weight: bfloat16 [32, 5632, 2048], P('req', 'tp'), as said below
Outputs:
- residual_out: bfloat16 [8192, 2048], P('req', 'tp')
- normed_out: bfloat16 [8192, 2048], P('req', 'tp')
Inputs may be any that keep to these rules, and one draw needn't show every extreme that they name: `routes`: each row names 2 different experts; in the rows of one index of req no expert is named by more than 128 rows, a bound that some block reaches. `gate_weight`: index r holds expert r % 8. `up_weight`: index r holds expert r % 8. `down_weight`: index r holds expert r % 8.
All inputs are finite; a program needn't handle non-finite values.
Results may differ from a plain program's by a relative error of at most 0.007.
Values may be sent and summed in bfloat16 or wider, within the bound.
No kernel may reach another device: no remote copies, remote signals or barrier semaphores. Data moves between devices by JAX's collectives and lax.ppermute only.
A program may use at most 128 MiB of HBM per device.

v0:
```python
import jax
import jax.numpy as jnp
from jax import lax
from jax.sharding import PartitionSpec as P

E = 8
CAP = 128
epsilon = 1e-05


def shards(hidden, routes, route_weights, pre_gain, out_gain, gate_weight, up_weight, down_weight):
    row_count, col_part = hidden.shape
    tp_count = lax.axis_size("tp")
    req_count = lax.axis_size("req")
    full_width = col_part * tp_count
    copies = req_count // E
    slot_count = CAP // copies
    stream = hidden.astype(jnp.float32)
    whole_rows = lax.all_gather(hidden, "tp", axis=1, tiled=True).astype(jnp.float32)
    meansq = jnp.sum(whole_rows * whole_rows, axis=1) / full_width
    normed_in = (whole_rows * lax.rsqrt(meansq + epsilon)[:, None] * pre_gain[None, :]).astype(
        jnp.bfloat16
    )
    send_cols = normed_in.shape[1]
    chosen = routes.reshape(-1)
    onehot = (chosen[:, None] == jnp.arange(E, dtype=jnp.int32)[None, :]).astype(jnp.int32)
    slot_rank = jnp.sum((jnp.cumsum(onehot, axis=0) - 1) * onehot, axis=1)
    position = chosen * CAP + slot_rank
    entry_rows = jnp.arange(chosen.shape[0], dtype=jnp.int32) // routes.shape[1]
    slot_row = jnp.zeros((E * CAP,), jnp.int32).at[position].set(entry_rows)
    slot_live = jnp.zeros((E * CAP,), jnp.bool_).at[position].set(True)
    outgoing = jnp.where(slot_live[:, None], normed_in[slot_row], jnp.zeros((), jnp.bfloat16))
    outgoing = outgoing.reshape(E, slot_count, copies, send_cols).transpose(2, 0, 1, 3)
    outgoing = outgoing.reshape(req_count, slot_count, send_cols)
    pieces = lax.all_to_all(outgoing, "req", split_axis=0, concat_axis=0, tiled=True)
    sources, items, widths = pieces.shape
    flat_rows = pieces.reshape(sources * items, widths)
    gate_val = jnp.dot(flat_rows, gate_weight[0], preferred_element_type=jnp.float32)
    up_val = jnp.dot(flat_rows, up_weight[0], preferred_element_type=jnp.float32)
    activ = (jax.nn.silu(gate_val) * up_val).astype(jnp.bfloat16)
    partial_out = jnp.dot(activ, down_weight[0], preferred_element_type=jnp.float32)
    partial_out = lax.optimization_barrier(partial_out.astype(jnp.bfloat16)).astype(jnp.float32)
    summed = lax.psum_scatter(
        partial_out.reshape(sources, items, widths).astype(jnp.bfloat16),
        "tp",
        scatter_dimension=2,
        tiled=True,
    )
    returned = lax.all_to_all(summed, "req", split_axis=0, concat_axis=0, tiled=True)
    returned = returned.reshape(copies, E, slot_count, col_part).transpose(1, 2, 0, 3)
    returned = returned.reshape(E * CAP, col_part)
    picked = returned[position].reshape(row_count, routes.shape[1], col_part).astype(jnp.float32)
    mixed = jnp.sum(picked * route_weights[:, :, None], axis=1)
    total_stream = stream + mixed
    out_sums = lax.psum(jnp.sum(total_stream * total_stream, axis=1), "tp")
    normed_out = (
        total_stream * lax.rsqrt(out_sums / full_width + epsilon)[:, None] * out_gain[None, :]
    )
    return (total_stream.astype(jnp.bfloat16), normed_out.astype(jnp.bfloat16))


def solution(mesh):
    return jax.shard_map(
        shards,
        mesh=mesh,
        in_specs=(
            P("req", "tp"),
            P("req", None),
            P("req", None),
            P(),
            P("tp"),
            P("req", None, "tp"),
            P("req", None, "tp"),
            P("req", "tp", None),
        ),
        out_specs=(P("req", "tp"), P("req", "tp")),
        check_vma=False,
    )
```

profile of v0, /device:TPU:0, one launch (start us, length us, event | category | flops | bytes accessed | tf_op | source)
XLA Modules:
  0.0 241.1 jit_solution(10688515270769743538)
XLA Ops:
  7.2 0.0 all-gather.2.cloned.1.call-start
  7.2 0.7 all-gather.2.cloned.1.call-update
  7.9 0.0 reduce-scatter.2.cloned.1.call-start
  7.9 0.8 copy.13
  8.8 0.1 eq.29
  8.9 0.1 eq.25
  9.1 1.1 reduce-window.6
  10.2 0.2 slice_reduce_fusion
  10.5 0.7 broadcast_multiply_fusion
  11.2 0.1 copy.12
  11.3 0.1 mul.74
  11.5 0.1 fusion.20
  11.6 2.4 %scatter_custom_fusion.1 = s32[1024]{0:T(1024)S(1)} fusion(s32[512]{0:T(512)S(1)} %bitcast.42, s32[512]{0:T(512)S(1)} %add_select_fusion, s32[]{:T(128)} %constant.37.clone.1), kind=kCustom, calls=%fused_computation.41 | custom fusion | bytes 4100 | tf_op jit(solution)/shard_map/scatter | solution.py:30
  14.0 2.4 %scatter_custom_fusion = pred[1024]{0:T(1024)(128)(4,1)S(1)} fusion(s32[512]{0:T(512)S(1)} %bitcast.43, pred[512]{0:T(512)(128)(4,1)S(1)} %broadcast.99, pred[]{:T(512)} %constant.20.clone.1), kind=kCustom, calls=%fused_computation.44 | custom fusion | bytes 1025 | tf_op jit(solution)/shard_map/scatter | solution.py:31
  16.5 0.2 broadcast_in_dim.35
  16.6 0.1 copy.15
  16.8 19.4 %all-gather.2.cloned.1.call-done = bf16[256,2048]{1,0:T(8,128)(2,1)} async-done(((bf16[256,512]{1,0:T(8,128)(2,1)}), bf16[256,2048]{1,0:T(8,128)(2,1)}) %all-gather.2.cloned.1.call-update) | async-done | bytes 1048592 | tf_op jit(solution)/shard_map/all_gather | solution.py:19
  36.1 1.5 fusion.16
  37.7 1.5 fusion.18
  39.2 6.0 %gather_fusion = bf16[1024,2048]{1,0:T(8,128)(2,1)} fusion(bf16[256,2048]{1,0:T(8,128)(2,1)S(1)} %fusion.18, s32[1024]{0:T(1024)S(1)} %fusion.22), kind=kCustom, calls=%fused_computation | custom fusion | bytes 8392704 | tf_op jit(solution)/shard_map/gather | solution.py:32
  45.2 7.2 %gather.9 = bf16[8,32,4,2048]{3,2,1,0:T(4,128)(2,1)} reshape(bf16[1024,2048]{1,0:T(8,128)(2,1)} %gather_fusion) | data formatting | bytes 8388608 | tf_op jit(solution)/shard_map/gather | solution.py:32
  52.4 8.5 %copy_select_fusion = bf16[8,32,4,2048]{3,1,0,2:T(8,128)(2,1)S(1)} fusion(bf16[8,32,4,2048]{3,2,1,0:T(4,128)(2,1)} %gather.9, pred[8,32,4]{1,0,2:T(8,128)(4,1)S(1)} %copy.15), kind=kLoop, calls=%fused_computation.11 | loop fusion | flops 2097152 | bytes 8389632 | tf_op jit(solution)/shard_map/jit(_where)/select_n | solution.py:32
  60.9 57.5 %all_to_all.10 = bf16[32,32,2048]{2,1,0:T(8,128)(2,1)S(1)} all-to-all(bf16[32,32,2048]{2,1,0:T(8,128)(2,1)S(1)} %bitcast.36), channel_id=1, replica_groups=mesh['req'=32,'tp'=4] {'req'}, dimensions={0} | all-to-all | bytes 8388608 | tf_op jit(solution)/shard_map/all_to_all | solution.py:35
  118.4 0.0 copy-start
  118.4 2.1 copy-done
  120.5 10.2 %fusion.4 = f32[1024,1408]{1,0:T(8,128)} fusion(bf16[1024,2048]{1,0:T(8,128)(2,1)S(1)} %bitcast.38, bf16[1,2048,1408]{2,1,0:T(8,128)(2,1)} %param.13), kind=kOutput, calls=%fused_computation.8 | convolution fusion | flops 5905580032 | bytes 15728640 | tf_op jit(solution)/shard_map/dot_general | solution.py:38
  130.8 20.6 %fusion.10 = bf16[1024,2048]{1,0:T(8,128)(2,1)} fusion(bf16[1,1408,2048]{2,1,0:T(8,128)(2,1)} %param.15, f32[1024,1408]{1,0:T(8,128)} %fusion.4, bf16[1024,2048]{1,0:T(8,128)(2,1)} %bitcast.39, bf16[1,2048,1408]{2,1,0:T(8,128)(2,1)} %param.14), kind=kOutput, calls=%fused_computation.12 | convolution fusion | flops 11821907968 | bytes 25690112 | tf_op jit(solution)/shard_map/dot_general | solution.py:41
  151.4 0.0 copy-start.2
  151.4 0.0 reduce-scatter.2.cloned.1.call-update
  151.4 44.1 %reduce-scatter.2.cloned.1.call-done = bf16[32,32,512]{2,1,0:T(8,128)(2,1)} async-done(((bf16[32,32,2048]{2,1,0:T(8,128)(2,1)}), bf16[32,32,512]{2,1,0:T(8,128)(2,1)}) %reduce-scatter.2.cloned.1.call-update) | async-done | bytes 1048592 | tf_op jit(solution)/shard_map/reduce_scatter | solution.py:43
  195.5 7.2 %all-to-all-start.1 = ((bf16[32,32,512]{2,1,0:T(8,128)(2,1)}), bf16[32,32,512]{2,1,0:T(8,128)(2,1)S(1)}, u32[]{:S(2)}, u32[]{:S(2)}) async-start(bf16[32,32,512]{2,1,0:T(8,128)(2,1)} %reduce-scatter.2.cloned.1.call-done), calls=%async_computation.2 | async-start | bytes 2097152 | tf_op jit(solution)/shard_map/all_to_all | solution.py:49
  202.8 0.0 copy-done.2
  202.8 0.1 copy.18
  202.9 16.6 %all-to-all-done.1 = bf16[32,32,512]{2,1,0:T(8,128)(2,1)S(1)} async-done(((bf16[32,32,512]{2,1,0:T(8,128)(2,1)}), bf16[32,32,512]{2,1,0:T(8,128)(2,1)S(1)}, u32[]{:S(2)}, u32[]{:S(2)}) %all-to-all-start.1) | async-done | bytes 1048608 | tf_op jit(solution)/shard_map/all_to_all | solution.py:49
  219.6 0.8 copy.21
  220.4 0.3 reshape.90
  220.7 0.0 copy-start.1
  220.7 0.0 copy-start.3
  220.7 2.0 gather_fusion.1
  222.7 0.7 reshape.91
  223.4 1.3 multiply_reduce_fusion
  224.7 0.0 copy-done.1
  224.7 0.1 multiply_reduce_fusion.1
  224.8 8.6 %psum.7 = f32[256]{0:T(256)S(1)} all-reduce(f32[256]{0:T(256)S(1)} %multiply_reduce_fusion.1), channel_id=1, replica_groups=mesh['req'=32,'tp'=4] {'tp'}, use_global_device_ids=true, to_apply=%region_9.10 | all-reduce | flops 256 | bytes 2048 | tf_op jit(solution)/shard_map/psum | solution.py:55
  233.4 0.0 copy-done.3
  233.4 0.8 multiply_convert_fusion.1
  (10 shorter events, 0.1 us)
Async XLA Ops:
  7.2 29.0 %all-gather.2.cloned.1.call-start = ((), (), s32[]{:S(2)}) async-start(), calls=%async_computation.3 | async-start | bytes 1310720 | tf_op jit(solution)/shard_map/all_gather | solution.py:19
  7.9 187.6 %reduce-scatter.2.cloned.1.call-start = ((), (), s32[]{:S(2)}) async-start(), calls=%async_computation.4 | async-start | bytes 5242880 | tf_op jit(solution)/shard_map/reduce_scatter | solution.py:43
  118.4 2.1 copy-start
  151.4 51.4 %copy-start.2 = (f32[256,2]{0,1:T(2,128)S(1)}, f32[256,2]{0,1:T(2,128)}, u32[]{:S(2)}) copy-start(f32[256,2]{0,1:T(2,128)} %param.10) | copy-start | bytes 6148
  195.5 24.1 %all-to-all-start.1 = ((bf16[32,32,512]{2,1,0:T(8,128)(2,1)}), bf16[32,32,512]{2,1,0:T(8,128)(2,1)S(1)}, u32[]{:S(2)}, u32[]{:S(2)}) async-start(bf16[32,32,512]{2,1,0:T(8,128)(2,1)} %reduce-scatter.2.cloned.1.call-done), calls=%async_computation.2 | async-start | bytes 2097152 | tf_op jit(solution)/shard_map/all_to_all | solution.py:49
  220.7 4.0 %copy-start.1 = (bf16[256,512]{1,0:T(8,128)(2,1)S(1)}, bf16[256,512]{1,0:T(8,128)(2,1)}, u32[]{:S(2)}) copy-start(bf16[256,512]{1,0:T(8,128)(2,1)} %param.8) | copy-start | bytes 786436
  220.7 12.7 %copy-start.3 = (f32[512]{0:T(512)S(1)}, f32[512]{0:T(512)}, u32[]{:S(2)}) copy-start(f32[512]{0:T(512)} %param.12) | copy-start | bytes 6148
Sparse Core Ops, SparseCore 0:
  9.7 26.4 all-gather.1
  151.5 43.9 reduce-scatter.1
where the time goes:
time: 242 us; the launch traced here: 241 us
  waiting for transfers between devices  80.8 us (33%)
  blocking collectives  66.1 us (27%)
  matrix products  30.9 us (13%)
  local copies, waits for them, and re-layouts  26 us (11%)
  other arithmetic  15.8 us (7%)
  between operations  14.2 us (6%)
  starting transfers between devices  7.31 us (3%)
    all_to_all x1, blocking collectives, shards(): lax.all_to_all(outgoing, 'req', split_axis=0, concat_axis=0, tiled=True)  57.5 us
    reduce_scatter x1, waiting for transfers between devices, shards(): lax.psum_scatter(partial_out.reshape(sources, items, widths).astype(jnp.b...  44.1 us
    dot_general x1, matrix products, shards(): jnp.dot(activ, down_weight[0], preferred_element_type=jnp.float32)  20.6 us
    all_gather x1, waiting for transfers between devices, shards(): lax.all_gather(hidden, 'tp', axis=1, tiled=True).astype(jnp.float32)  19.4 us
    all_to_all x1, waiting for transfers between devices, shards(): lax.all_to_all(summed, 'req', split_axis=0, concat_axis=0, tiled=True)  16.6 us
    gather x2, local copies, waits for them, and re-layouts, shards(): normed_in[slot_row]  13.2 us
    dot_general x1, matrix products, shards(): jnp.dot(flat_rows, gate_weight[0], preferred_element_type=jnp.float32)  10.2 us
    psum x1, blocking collectives, shards(): out_sums = lax.psum(jnp.sum(total_stream * total_stream, axis=1), 'tp')  8.58 us
  transfers between devices with their start and end apart: 3, of which 3 were waited for; matrix products, arithmetic and copies ran while one was open for 4% of the time, Pallas kernels for 0%

commit v1 on v0

--- a/solution.py
+++ b/solution.py
@@ -8,6 +8,11 @@
 epsilon = 1e-05
 
 
+def exchange_gather(shard, axis, along):
+    repeated = jnp.stack([shard] * lax.axis_size(axis))
+    return jnp.concatenate(lax.all_to_all(repeated, axis, 0, 0), axis=along)
+
+
 def shards(hidden, routes, route_weights, pre_gain, out_gain, gate_weight, up_weight, down_weight):
     row_count, col_part = hidden.shape
     tp_count = lax.axis_size("tp")
@@ -16,7 +21,7 @@
     copies = req_count // E
     slot_count = CAP // copies
     stream = hidden.astype(jnp.float32)
-    whole_rows = lax.all_gather(hidden, "tp", axis=1, tiled=True).astype(jnp.float32)
+    whole_rows = exchange_gather(hidden, "tp", 1).astype(jnp.float32)
     meansq = jnp.sum(whole_rows * whole_rows, axis=1) / full_width
     normed_in = (whole_rows * lax.rsqrt(meansq + epsilon)[:, None] * pre_gain[None, :]).astype(
         jnp.bfloat16

time: 242 us -> 232 us (0.959)
  waiting for transfers between devices: 80.8 us -> 66.2 us
  starting transfers between devices: 7.31 us -> 11.8 us
    all_gather x1 -> x0, waiting for transfers between devices: 19.4 us -> none  [shards(): lax.all_gather(hidden, 'tp', axis=1, tiled=True).astype(jnp.float32)]
    all_to_all x0 -> x1, waiting for transfers between devices: none -> 6.27 us  [exchange_gather(): return jnp.concatenate(lax.all_to_all(repeated, axis, 0, 0), axis=along)]
    all_to_all x0 -> x1, starting transfers between devices: none -> 4.55 us  [exchange_gather(): return jnp.concatenate(lax.all_to_all(repeated, axis, 0, 0), axis=along)]
where the time goes in v1:
time: 232 us
  blocking collectives  67.1 us (29%)
  waiting for transfers between devices  66.2 us (29%)
  matrix products  30.9 us (13%)
  local copies, waits for them, and re-layouts  28.2 us (12%)
  between operations  14.2 us (6%)
  other arithmetic  13.6 us (6%)
  starting transfers between devices  11.8 us (5%)
    all_to_all x1, blocking collectives, shards(): lax.all_to_all(outgoing, 'req', split_axis=0, concat_axis=0, tiled=True)  58.5 us
    reduce_scatter x1, waiting for transfers between devices, shards(): lax.psum_scatter(partial_out.reshape(sources, items, widths).astype(jnp.b...  43.2 us
    dot_general x1, matrix products, shards(): jnp.dot(activ, down_weight[0], preferred_element_type=jnp.float32)  20.6 us
    all_to_all x1, waiting for transfers between devices, shards(): lax.all_to_all(summed, 'req', split_axis=0, concat_axis=0, tiled=True)  16.6 us
    gather x2, local copies, waits for them, and re-layouts, shards(): normed_in[slot_row]  13.2 us
    dot_general x1, matrix products, shards(): jnp.dot(flat_rows, gate_weight[0], preferred_element_type=jnp.float32)  10.2 us
    psum x1, blocking collectives, shards(): out_sums = lax.psum(jnp.sum(total_stream * total_stream, axis=1), 'tp')  8.58 us
    select_n x1, other arithmetic, shards(): jnp.where(slot_live[:, None], normed_in[slot_row], jnp.zeros((), jnp.bflo...  8.47 us
  transfers between devices with their start and end apart: 3, of which 3 were waited for; matrix products, arithmetic and copies ran while one was open for 4% of the time, Pallas kernels for 0%

profile of v1, /device:TPU:0, one launch (start us, length us, event | category | flops | bytes accessed | tf_op | source)
XLA Modules:
  0.0 231.9 jit_solution(6911622786086220568)
XLA Ops:
  7.2 2.0 stack.2
  9.2 4.5 %all-to-all-start = ((bf16[4,256,512]{2,1,0:T(8,128)(2,1)}), bf16[4,256,512]{2,1,0:T(8,128)(2,1)S(1)}, u32[]{:S(2)}, u32[]{:S(2)}) async-start(bf16[4,256,512]{2,1,0:T(8,128)(2,1)} %stack.2), calls=%async_computation | async-start | bytes 2097152 | tf_op jit(solution)/shard_map/all_to_all | solution.py:13
  13.7 0.0 reduce-scatter.2.cloned.1.call-start
  13.7 0.8 copy.20
  14.6 0.1 eq.29
  14.7 0.1 eq.25
  14.8 0.7 broadcast_multiply_fusion
  15.5 1.1 reduce-window.6
  16.7 0.2 slice_reduce_fusion
  16.9 0.1 copy.19
  17.1 0.1 mul.76
  17.2 0.1 fusion.18
  17.3 2.4 %scatter_custom_fusion.1 = s32[1024]{0:T(1024)S(1)} fusion(s32[512]{0:T(512)S(1)} %bitcast.47, s32[512]{0:T(512)S(1)} %add_select_fusion, s32[]{:T(128)} %constant.37.clone.1), kind=kCustom, calls=%fused_computation.40 | custom fusion | bytes 4100 | tf_op jit(solution)/shard_map/scatter | solution.py:35
  19.8 2.4 %scatter_custom_fusion = pred[1024]{0:T(1024)(128)(4,1)S(1)} fusion(s32[512]{0:T(512)S(1)} %bitcast.48, pred[512]{0:T(512)(128)(4,1)S(1)} %broadcast.101, pred[]{:T(512)} %constant.20.clone.1), kind=kCustom, calls=%fused_computation.43 | custom fusion | bytes 1025 | tf_op jit(solution)/shard_map/scatter | solution.py:36
  22.2 0.2 broadcast_in_dim.35
  22.4 0.1 copy.22
  22.5 0.0 copy-start.2
  22.6 6.3 %all-to-all-done = bf16[4,256,512]{2,1,0:T(8,128)(2,1)S(1)} async-done(((bf16[4,256,512]{2,1,0:T(8,128)(2,1)}), bf16[4,256,512]{2,1,0:T(8,128)(2,1)S(1)}, u32[]{:S(2)}, u32[]{:S(2)}) %all-to-all-start) | async-done | bytes 1048608 | tf_op jit(solution)/shard_map/all_to_all | solution.py:13
  28.8 0.3 convert_bitcast_fusion
  29.1 0.2 copy.27
  29.4 0.3 fusion.16
  29.7 0.0 copy-done.2
  29.7 0.2 multiply_convert_fusion.1
  29.9 6.0 %gather_fusion = bf16[1024,2048]{1,0:T(8,128)(2,1)} fusion(bf16[256,2048]{1,0:T(8,128)(2,1)S(1)} %multiply_convert_fusion.1, s32[1024]{0:T(1024)S(1)} %fusion.20), kind=kCustom, calls=%fused_computation | custom fusion | bytes 8392704 | tf_op jit(solution)/shard_map/gather | solution.py:37
  35.9 7.2 %gather.9 = bf16[8,32,4,2048]{3,2,1,0:T(4,128)(2,1)} reshape(bf16[1024,2048]{1,0:T(8,128)(2,1)} %gather_fusion) | data formatting | bytes 8388608 | tf_op jit(solution)/shard_map/gather | solution.py:37
  43.1 8.5 %copy_select_fusion = bf16[8,32,4,2048]{3,1,0,2:T(8,128)(2,1)S(1)} fusion(bf16[8,32,4,2048]{3,2,1,0:T(4,128)(2,1)} %gather.9, pred[8,32,4]{1,0,2:T(8,128)(4,1)S(1)} %copy.22), kind=kLoop, calls=%fused_computation.11 | loop fusion | flops 2097152 | bytes 8389632 | tf_op jit(solution)/shard_map/jit(_where)/select_n | solution.py:37
  51.6 58.5 %all_to_all.15 = bf16[32,32,2048]{2,1,0:T(8,128)(2,1)S(1)} all-to-all(bf16[32,32,2048]{2,1,0:T(8,128)(2,1)S(1)} %bitcast.40), channel_id=1, replica_groups=mesh['req'=32,'tp'=4] {'req'}, dimensions={0} | all-to-all | bytes 8388608 | tf_op jit(solution)/shard_map/all_to_all | solution.py:40
  110.1 0.0 copy-start
  110.1 2.1 copy-done
  112.2 10.2 %fusion.4 = f32[1024,1408]{1,0:T(8,128)} fusion(bf16[1024,2048]{1,0:T(8,128)(2,1)S(1)} %bitcast.43, bf16[1,2048,1408]{2,1,0:T(8,128)(2,1)} %param.13), kind=kOutput, calls=%fused_computation.8 | convolution fusion | flops 5905580032 | bytes 15728640 | tf_op jit(solution)/shard_map/dot_general | solution.py:43
  122.4 20.6 %fusion.10 = bf16[1024,2048]{1,0:T(8,128)(2,1)} fusion(bf16[1,1408,2048]{2,1,0:T(8,128)(2,1)} %param.15, f32[1024,1408]{1,0:T(8,128)} %fusion.4, bf16[1024,2048]{1,0:T(8,128)(2,1)} %bitcast.44, bf16[1,2048,1408]{2,1,0:T(8,128)(2,1)} %param.14), kind=kOutput, calls=%fused_computation.12 | convolution fusion | flops 11821907968 | bytes 25690112 | tf_op jit(solution)/shard_map/dot_general | solution.py:46
  143.0 0.0 copy-start.3
  143.0 0.0 reduce-scatter.2.cloned.1.call-update
  143.1 43.2 %reduce-scatter.2.cloned.1.call-done = bf16[32,32,512]{2,1,0:T(8,128)(2,1)} async-done(((bf16[32,32,2048]{2,1,0:T(8,128)(2,1)}), bf16[32,32,512]{2,1,0:T(8,128)(2,1)}) %reduce-scatter.2.cloned.1.call-update) | async-done | bytes 1048592 | tf_op jit(solution)/shard_map/reduce_scatter | solution.py:48
  186.3 7.2 %all-to-all-start.2 = ((bf16[32,32,512]{2,1,0:T(8,128)(2,1)}), bf16[32,32,512]{2,1,0:T(8,128)(2,1)S(1)}, u32[]{:S(2)}, u32[]{:S(2)}) async-start(bf16[32,32,512]{2,1,0:T(8,128)(2,1)} %reduce-scatter.2.cloned.1.call-done), calls=%async_computation.3 | async-start | bytes 2097152 | tf_op jit(solution)/shard_map/all_to_all | solution.py:54
  193.5 0.0 copy-done.3
  193.5 0.1 copy.26
  193.7 16.6 %all-to-all-done.2 = bf16[32,32,512]{2,1,0:T(8,128)(2,1)S(1)} async-done(((bf16[32,32,512]{2,1,0:T(8,128)(2,1)}), bf16[32,32,512]{2,1,0:T(8,128)(2,1)S(1)}, u32[]{:S(2)}, u32[]{:S(2)}) %all-to-all-start.2) | async-done | bytes 1048608 | tf_op jit(solution)/shard_map/all_to_all | solution.py:54
  210.4 0.8 copy.30
  211.2 0.3 reshape.96
  211.5 0.0 copy-start.1
  211.5 0.0 copy-start.4
  211.5 2.0 gather_fusion.1
  213.5 0.7 reshape.98
  214.1 1.3 multiply_reduce_fusion
  215.5 0.0 copy-done.1
  215.5 0.1 multiply_reduce_fusion.1
  215.6 8.6 %psum.7 = f32[256]{0:T(256)S(1)} all-reduce(f32[256]{0:T(256)S(1)} %multiply_reduce_fusion.1), channel_id=1, replica_groups=mesh['req'=32,'tp'=4] {'tp'}, use_global_device_ids=true, to_apply=%region_9.10 | all-reduce | flops 256 | bytes 2048 | tf_op jit(solution)/shard_map/psum | solution.py:60
  224.2 0.0 copy-done.4
  224.2 0.8 multiply_convert_fusion.2
  (10 shorter events, 0.1 us)
Async XLA Ops:
  9.2 19.6 %all-to-all-start = ((bf16[4,256,512]{2,1,0:T(8,128)(2,1)}), bf16[4,256,512]{2,1,0:T(8,128)(2,1)S(1)}, u32[]{:S(2)}, u32[]{:S(2)}) async-start(bf16[4,256,512]{2,1,0:T(8,128)(2,1)} %stack.2), calls=%async_computation | async-start | bytes 2097152 | tf_op jit(solution)/shard_map/all_to_all | solution.py:13
  13.7 172.6 %reduce-scatter.2.cloned.1.call-start = ((), (), s32[]{:S(2)}) async-start(), calls=%async_computation.4 | async-start | bytes 5242880 | tf_op jit(solution)/shard_map/reduce_scatter | solution.py:48
  22.5 7.1 %copy-start.2 = (f32[2048]{0:T(1024)S(1)}, f32[2048]{0:T(1024)}, u32[]{:S(2)}) copy-start(f32[2048]{0:T(1024)} %param.11) | copy-start | bytes 24580
  110.1 2.1 copy-start
  143.0 50.5 %copy-start.3 = (f32[256,2]{0,1:T(2,128)S(1)}, f32[256,2]{0,1:T(2,128)}, u32[]{:S(2)}) copy-start(f32[256,2]{0,1:T(2,128)} %param.10) | copy-start | bytes 6148
  186.3 24.0 %all-to-all-start.2 = ((bf16[32,32,512]{2,1,0:T(8,128)(2,1)}), bf16[32,32,512]{2,1,0:T(8,128)(2,1)S(1)}, u32[]{:S(2)}, u32[]{:S(2)}) async-start(bf16[32,32,512]{2,1,0:T(8,128)(2,1)} %reduce-scatter.2.cloned.1.call-done), calls=%async_computation.3 | async-start | bytes 2097152 | tf_op jit(solution)/shard_map/all_to_all | solution.py:54
  211.5 4.0 %copy-start.1 = (bf16[256,512]{1,0:T(8,128)(2,1)S(1)}, bf16[256,512]{1,0:T(8,128)(2,1)}, u32[]{:S(2)}) copy-start(bf16[256,512]{1,0:T(8,128)(2,1)} %param.8) | copy-start | bytes 786436
  211.5 12.7 %copy-start.4 = (f32[512]{0:T(512)S(1)}, f32[512]{0:T(512)}, u32[]{:S(2)}) copy-start(f32[512]{0:T(512)} %param.12) | copy-start | bytes 6148
Sparse Core Ops, SparseCore 0:
  143.2 43.0 reduce-scatter.1
